TPU v7x, 256 devices: a whole 4x4x8 slice. The times are simulated.
256 devices in a mesh: dp: 8 (over z), expert: 32 (over y, x, core).
Axes of the slice: x: 4, y: 4, z: 8, core: 2. Of those that a mesh axis runs over, the one named last changes fastest.
Arguments:
- tokens: bfloat16 [32, 16, 7168], P('expert', 'dp'), may hold values from -6 to 6
- tangent: bfloat16 [32, 16, 7168], P('expert', 'dp'), may hold values from -52 to 52
- route_ids: int32 [32, 16, 8], P('expert', 'dp'), may hold values from 0 to 31, all different within a row; in each aligned block of 16 rows (0 to 15, 16 to 31, ..., all dimensions but the last counted through in order) at most 8 rows name the same one
- gate_fixed: int32 [32, 16, 8], P('expert', 'dp'), may hold values from 4096 to 65535
- gate_proj: bfloat16 [32, 7168, 2048], P('expert', None, 'dp'), may hold values from -0.0625 to 0.0625
- up_proj: bfloat16 [32, 7168, 2048], P('expert', None, 'dp'), may hold values from -0.0625 to 0.0625
- down_proj: bfloat16 [32, 2048, 7168], P('expert', 'dp'), may hold values from -0.125 to 0.125
Outputs:
- next_tangent: bfloat16 [32, 16, 7168], P('expert', 'dp')
- lipschitz: float32 [], replicated
Inputs may be any that keep to these rules, and one draw needn't show every extreme that they name: `route_ids`: each token names 8 different experts; within one group of 16 tokens no expert is named by more than 8 tokens.
All inputs are finite; a program needn't handle non-finite values.
Results may differ from a plain program's by a relative error of at most 0.0065.
Values may be sent and summed in bfloat16 or wider, within the bound.
No kernel may reach another device: no remote copies, remote signals or barrier semaphores. Data moves between devices by JAX's collectives and lax.ppermute only.
A program may use at most 128 MiB of HBM per device.

v0:
```python
import jax
import jax.numpy as jnp
from jax import lax
from jax.sharding import PartitionSpec as P

BF16 = jnp.bfloat16
F32 = jnp.float32


def silu_parts(gate_pre):
    sigmoid_val = jax.nn.sigmoid(gate_pre)
    return (gate_pre * sigmoid_val, sigmoid_val * (1.0 + gate_pre * (1.0 - sigmoid_val)))


def contract_last(left, right):
    return lax.dot_general(left, right, (((1,), (1,)), ((), ())), preferred_element_type=F32)


def exchange(value):
    return lax.all_to_all(value, "expert", split_axis=0, concat_axis=0, tiled=True)


def body(tokens, tangent, route_ids, gate_fixed, gate_proj, up_proj, down_proj):
    model_width = tokens.shape[2]
    tok_dev = tokens.shape[1]
    top_count = route_ids.shape[2]
    experts = lax.axis_size("expert")
    gates_local = gate_fixed[0]
    pieces = [
        tokens[0],
        tangent[0],
        route_ids[0].astype(BF16),
        (gates_local // 256).astype(BF16),
        (gates_local % 256).astype(BF16),
    ]
    width = 2 * model_width + 3 * top_count
    pad = -width % 128
    if pad:
        pieces.append(jnp.zeros((tok_dev, pad), BF16))
    packed = jnp.concatenate(pieces, axis=1)
    col = lax.all_gather(packed, "dp", axis=0, tiled=True)
    col_count = col.shape[0]
    meta = col[:, 2 * model_width : width].astype(jnp.int32)
    col_ids = meta[:, :top_count]
    col_gates = meta[:, top_count : 2 * top_count] * 256 + meta[:, 2 * top_count :]
    col_pair = jnp.concatenate(
        [col[:, :model_width], col[:, model_width : 2 * model_width]], axis=0
    )
    capacity = min(col_count, 2 * col_count * top_count // experts)
    slot_total = experts * capacity
    flat_ids = col_ids.reshape(-1)
    experts_all = jnp.arange(experts, dtype=jnp.int32)
    onehot = (flat_ids[:, None] == experts_all[None, :]).astype(jnp.int32)
    earlier = jnp.cumsum(onehot, axis=0) - onehot
    slot_place = jnp.sum(earlier * onehot, axis=1)
    target = flat_ids * capacity + slot_place
    places = jnp.arange(slot_total, dtype=jnp.int32)
    matches = target[:, None] == places[None, :]
    route_f = jnp.sum(matches.reshape(col_count, top_count, slot_total), axis=1).astype(F32).T
    route_map = route_f.astype(BF16)
    gate_vals = col_gates.reshape(-1).astype(F32) / 65536.0
    combine_map = jnp.sum(
        jnp.where(matches, gate_vals[:, None], 0.0).reshape(col_count, top_count, slot_total),
        axis=1,
    )
    eye2 = jnp.eye(2, dtype=F32)
    pair_map = (
        (route_f.reshape(experts, 1, capacity, 1, col_count) * eye2.reshape(1, 2, 1, 2, 1))
        .reshape(experts * 2 * capacity, 2 * col_count)
        .astype(BF16)
    )
    send_pair = (
        jnp.dot(pair_map, col_pair, preferred_element_type=F32)
        .astype(BF16)
        .reshape(experts, 2 * capacity, model_width)
    )
    weight_gate = gate_proj[0]
    weight_up = up_proj[0]
    weight_down = down_proj[0]
    hidden_dev = weight_gate.shape[1]
    rows_pair = exchange(send_pair)
    groups_here = rows_pair.shape[0]
    flat_pair = rows_pair.reshape(-1, model_width)
    gate_both = jnp.dot(flat_pair, weight_gate, preferred_element_type=F32).reshape(
        groups_here, 2, capacity, hidden_dev
    )
    up_both = jnp.dot(flat_pair, weight_up, preferred_element_type=F32).reshape(
        groups_here, 2, capacity, hidden_dev
    )
    gate_pre = gate_both[:, 0].reshape(-1, hidden_dev)
    gate_dir = gate_both[:, 1].reshape(-1, hidden_dev)
    up_pre = up_both[:, 0].reshape(-1, hidden_dev)
    up_dir = up_both[:, 1].reshape(-1, hidden_dev)
    silu_value, silu_slope = silu_parts(gate_pre)
    jvp_hidden = (silu_slope * gate_dir * up_pre + silu_value * up_dir).astype(BF16)
    partial_value = jnp.dot(jvp_hidden, weight_down, preferred_element_type=F32)
    returned = exchange(partial_value.astype(BF16).reshape(groups_here, capacity, model_width))
    gate_coef = silu_slope * up_pre
    up_coef = silu_value
    product_part = jnp.dot(
        combine_map,
        returned.reshape(slot_total, -1).astype(F32),
        precision=lax.Precision.HIGHEST,
        preferred_element_type=F32,
    )
    product_bf = lax.psum(product_part, "dp").astype(BF16)
    send_prod = (
        jnp.dot(route_map, product_bf, preferred_element_type=F32)
        .astype(BF16)
        .reshape(experts, capacity, model_width)
    )
    received = exchange(send_prod)
    grad_hidden = contract_last(received.reshape(slot_total, model_width), weight_down)
    grad_gate = (grad_hidden * gate_coef).astype(BF16)
    grad_up = (grad_hidden * up_coef).astype(BF16)
    vjp_part = contract_last(grad_gate, weight_gate) + contract_last(grad_up, weight_up)
    returned_two = exchange(vjp_part.astype(BF16).reshape(experts, capacity, model_width))
    result_part = jnp.dot(
        combine_map,
        returned_two.reshape(slot_total, -1).astype(F32),
        precision=lax.Precision.HIGHEST,
        preferred_element_type=F32,
    )
    result = lax.psum_scatter(result_part, "dp", scatter_dimension=0, tiled=True)
    probe_f = tangent[0].astype(F32)
    probe_result, result_sq, probe_sq = lax.psum(
        (jnp.sum(probe_f * result), jnp.sum(result * result), jnp.sum(probe_f * probe_f)),
        ("dp", "expert"),
    )
    total_cells = lax.axis_size("dp") * lax.axis_size("expert") * tok_dev * model_width
    next_tangent = (result * lax.rsqrt(result_sq / total_cells + 1e-06)).astype(BF16)
    lipschitz = jnp.sqrt(probe_result / probe_sq)
    return (next_tangent[None], lipschitz)


def solution(mesh):
    return jax.shard_map(
        body,
        mesh=mesh,
        in_specs=(
            P("expert", "dp", None),
            P("expert", "dp", None),
            P("expert", "dp", None),
            P("expert", "dp", None),
            P("expert", None, "dp"),
            P("expert", None, "dp"),
            P("expert", "dp", None),
        ),
        out_specs=(P("expert", "dp", None), P()),
        check_vma=False,
    )
```

profile of v0, /device:TPU:1, one launch (start us, length us, event | category | flops | bytes accessed | tf_op | source)
XLA Modules:
  0.0 496.2 jit_solution(14524132102642386330)
XLA Ops:
  7.2 0.7 fusion.50
  7.9 0.7 convert_bitcast_fusion.1
  8.6 0.9 concatenate.6
  9.4 23.7 %all-gather = bf16[8,2,14464]{2,1,0:T(2,128)(2,1)S(1)} all-gather(bf16[1,2,14464]{2,1,0:T(2,128)(2,1)S(1)} %bitcast.125), channel_id=1, replica_groups=mesh['dp'=8,'expert'=32] {'dp'}, dimensions={0}, use_global_device_ids=true | all-gather | bytes 520704 | tf_op jit(solution)/shard_map/all_gather | solution.py:41
  33.1 0.2 reshape.97
  33.5 0.2 reduce_window_sum.11
  33.7 0.2 select_reduce_fusion.1
  34.2 0.2 multiply_convert_fusion
  34.5 0.1 convert_element_type.99
  34.6 2.0 convolution_convert_fusion
  36.7 98.5 %all_to_all.20 = bf16[32,16,7168]{2,1,0:T(8,128)(2,1)S(1)} all-to-all(bf16[32,16,7168]{2,1,0:T(8,128)(2,1)S(1)} %bitcast.123), channel_id=1, replica_groups=mesh['dp'=8,'expert'=32] {'expert'}, dimensions={0} | all-to-all | bytes 14680064 | tf_op jit(solution)/shard_map/all_to_all | solution.py:20
  135.2 2.1 fusion.6
  137.2 2.1 fusion.4
  139.3 3.1 fusion.1
  142.4 4.8 all-to-all-start.1
  147.4 44.9 %all-to-all-done.1 = bf16[32,8,7168]{2,1,0:T(8,128)(2,1)} async-done(((bf16[32,8,7168]{2,1,0:T(8,128)(2,1)}), bf16[32,8,7168]{2,1,0:T(8,128)(2,1)}, u32[]{:S(2)}, u32[]{:S(2)}) %all-to-all-start.1) | async-done | bytes 3670048 | tf_op jit(solution)/shard_map/all_to_all | solution.py:20
  192.3 3.6 fusion.14
  195.9 28.2 %all-reduce.6 = bf16[16,7168]{1,0:T(8,128)(2,1)S(1)} all-reduce(f32[16,7168]{1,0:T(8,128)S(1)} %fusion.14), channel_id=1, replica_groups=mesh['dp'=8,'expert'=32] {'dp'}, use_global_device_ids=true, to_apply=%region_4.5 | all-reduce | flops 114688 | bytes 688128 | tf_op jit(solution)/shard_map/psum | solution.py:106
  224.1 1.1 fusion.2
  225.3 57.6 %all_to_all.21 = bf16[32,8,7168]{2,1,0:T(8,128)(2,1)S(1)} all-to-all(bf16[32,8,7168]{2,1,0:T(8,128)(2,1)S(1)} %fusion.2), channel_id=1, replica_groups=mesh['dp'=8,'expert'=32] {'expert'}, dimensions={0} | all-to-all | bytes 7340032 | tf_op jit(solution)/shard_map/all_to_all | solution.py:20
  282.9 1.1 fusion.12
  284.0 0.9 copy-done.3
  284.9 1.2 fusion.19
  286.1 0.8 copy-done.5
  287.0 1.2 fusion.3
  288.1 48.9 %all_to_all.22 = bf16[32,8,7168]{2,1,0:T(8,128)(2,1)S(1)} all-to-all(bf16[32,8,7168]{2,1,0:T(8,128)(2,1)S(1)} %fusion.3), channel_id=1, replica_groups=mesh['dp'=8,'expert'=32] {'expert'}, dimensions={0} | all-to-all | bytes 7340032 | tf_op jit(solution)/shard_map/all_to_all | solution.py:20
  337.0 2.3 fusion.10
  339.4 0.6 dynamic-slice
  340.6 62.1 %all-reduce.5.cloned.1.call-done = f32[16,7168]{1,0:T(8,128)} async-done(((f32[16,7168]{1,0:T(8,128)}), f32[16,7168]{1,0:T(8,128)}) %all-reduce.5.cloned.1.call-update) | async-done | bytes 458768
  402.8 1.7 fusion.44
  404.5 80.1 %all-reduce.1 = (f32[]{:T(128)}, f32[]{:T(128)}, f32[]{:T(128)}) all-reduce(f32[]{:T(128)} %get-tuple-element.3, f32[]{:T(128)} %get-tuple-element.2, f32[]{:T(128)} %get-tuple-element.4), channel_id=1, replica_groups=mesh['dp'=8,'expert'=32] {'dp','expert'}, use_global_device_ids=true, to_apply=%region_7.8 | all-reduce | flops 3 | bytes 24 | tf_op jit(solution)/shard_map/psum | solution.py:126
  486.6 1.6 fusion.46
  (29 shorter events, 0.8 us)
Async XLA Ops:
  36.7 98.5 %copy-start.2 = (bf16[1,7168,256]{2,1,0:T(8,128)(2,1)S(1)}, bf16[1,7168,256]{2,1,0:T(8,128)(2,1)}, u32[]{:S(2)}) copy-start(bf16[1,7168,256]{2,1,0:T(8,128)(2,1)} %param.11) | copy-start | bytes 11010052
  135.2 2.1 copy-start.4
  137.2 2.1 copy-start
  142.4 50.0 %all-to-all-start.1 = ((bf16[32,8,7168]{2,1,0:T(8,128)(2,1)}), bf16[32,8,7168]{2,1,0:T(8,128)(2,1)}, u32[]{:S(2)}, u32[]{:S(2)}) async-start(bf16[32,8,7168]{2,1,0:T(8,128)(2,1)} %fusion.1), calls=%async_computation.1 | async-start | bytes 7340032 | tf_op jit(solution)/shard_map/all_to_all | solution.py:20
  147.2 255.6 %all-reduce.5.cloned.1.call-start = ((), (), s32[]{:S(2)}) async-start(), calls=%async_computation.4 | async-start | bytes 917504
  225.3 57.6 %copy-start.1 = (bf16[1,256,7168]{2,1,0:T(8,128)(2,1)S(1)}, bf16[1,256,7168]{2,1,0:T(8,128)(2,1)}, u32[]{:S(2)}) copy-start(bf16[1,256,7168]{2,1,0:T(8,128)(2,1)} %param.13) | copy-start | bytes 11010052
  282.9 2.0 copy-start.3
  284.9 2.0 copy-start.5
  337.0 2.4 copy-start.7
  337.0 65.7 %copy-start.6 = (bf16[1,2,7168]{2,1,0:T(2,128)(2,1)S(1)}, bf16[1,2,7168]{2,1,0:T(2,128)(2,1)}, u32[]{:S(2)}) copy-start(bf16[1,2,7168]{2,1,0:T(2,128)(2,1)} %param.8) | copy-start | bytes 86020
Sparse Core Ops, SparseCore 0:
  339.5 63.2 all-reduce.4
where the time goes:
time: 497 us; the launch traced here: 496 us
  blocking collectives  337 us (68%)
  waiting for transfers between devices  107 us (22%)
  matrix products  19.7 us (4%)
  between operations  18.1 us (4%)
  other arithmetic  5.68 us (1%)
    all_to_all x3, blocking collectives, exchange(): lax.all_to_all(value, 'expert', split_axis=0, concat_axis=0, tiled=True)  205 us
    psum x1, blocking collectives, body(): lax.psum((jnp.sum(probe_f * result), jnp.sum(result * result), jnp.sum(pr...  80.1 us
    unnamed x2, waiting for transfers between devices  62.1 us
    all_to_all x1, waiting for transfers between devices, exchange(): lax.all_to_all(value, 'expert', split_axis=0, concat_axis=0, tiled=True)  44.9 us
    psum x1, blocking collectives, body(): product_bf = lax.psum(product_part, 'dp').astype(BF16)  28.2 us
    all_gather x1, blocking collectives, body(): col = lax.all_gather(packed, 'dp', axis=0, tiled=True)  23.7 us
  transfers between devices with their start and end apart: 2, of which 2 were waited for; matrix products, arithmetic and copies ran while one was open for 0% of the time, Pallas kernels for 0%

commit v1 on v0

--- a/solution.py
+++ b/solution.py
@@ -38,7 +38,8 @@
     if pad:
         pieces.append(jnp.zeros((tok_dev, pad), BF16))
     packed = jnp.concatenate(pieces, axis=1)
-    col = lax.all_gather(packed, "dp", axis=0, tiled=True)
+    sent = jnp.stack([packed] * lax.axis_size("dp"))
+    col = jnp.concatenate(lax.all_to_all(sent, "dp", 0, 0), axis=0)
     col_count = col.shape[0]
     meta = col[:, 2 * model_width : width].astype(jnp.int32)
     col_ids = meta[:, :top_count]

time: 497 us -> 492 us (0.990)
  blocking collectives: 337 us -> 306 us
  waiting for transfers between devices: 107 us -> 123 us
  starting transfers between devices: 4.86 us -> 13.9 us
    all_gather x1 -> x0, blocking collectives: 23.7 us -> none  [body(): col = lax.all_gather(packed, 'dp', axis=0, tiled=True)]
    all_to_all x0 -> x1, waiting for transfers between devices: none -> 16.6 us  [body(): col = jnp.concatenate(lax.all_to_all(sent, 'dp', 0, 0), axis=0)]
    all_to_all x0 -> x1, starting transfers between devices: none -> 9 us  [body(): col = jnp.concatenate(lax.all_to_all(sent, 'dp', 0, 0), axis=0)]
    all_to_all x3, blocking collectives: 205 us -> 200 us  [exchange(): lax.all_to_all(value, 'expert', split_axis=0, concat_axis=0, tiled=True)]
  transfers between devices with their start and end apart: 2 -> 3, of which waited for: 2 -> 3; matrix products, arithmetic and copies ran while one was open for 0% -> 0% of each run, Pallas kernels for 0% -> 0%
where the time goes in v1:
time: 492 us; the launch traced here: 491 us
  blocking collectives  306 us (62%)
  waiting for transfers between devices  123 us (25%)
  matrix products  19.7 us (4%)
  between operations  18.1 us (4%)
  starting transfers between devices  13.9 us (3%)
  other arithmetic  5.68 us (1%)
    all_to_all x3, blocking collectives, exchange(): lax.all_to_all(value, 'expert', split_axis=0, concat_axis=0, tiled=True)  200 us
    psum x1, blocking collectives, body(): lax.psum((jnp.sum(probe_f * result), jnp.sum(result * result), jnp.sum(pr...  80.1 us
    unnamed x2, waiting for transfers between devices  61.3 us
    all_to_all x1, waiting for transfers between devices, exchange(): lax.all_to_all(value, 'expert', split_axis=0, concat_axis=0, tiled=True)  44.9 us
    psum x1, blocking collectives, body(): product_bf = lax.psum(product_part, 'dp').astype(BF16)  26.2 us
    all_to_all x1, waiting for transfers between devices, body(): col = jnp.concatenate(lax.all_to_all(sent, 'dp', 0, 0), axis=0)  16.6 us
  transfers between devices with their start and end apart: 3, of which 3 were waited for; matrix products, arithmetic and copies ran while one was open for 0% of the time, Pallas kernels for 0%

profile of v1, /device:TPU:1, one launch (start us, length us, event | category | flops | bytes accessed | tf_op | source)
XLA Modules:
  0.0 490.8 jit_solution(16833712536492034778)
XLA Ops:
  7.2 0.7 fusion.50
  7.9 0.7 convert_bitcast_fusion.1
  8.5 0.9 concatenate.6
  9.4 1.0 stack.2
  10.4 9.0 %all-to-all-start = ((bf16[8,2,14464]{2,1,0:T(2,128)(2,1)}), bf16[8,2,14464]{2,1,0:T(2,128)(2,1)S(1)}, u32[]{:S(2)}, u32[]{:S(2)}) async-start(bf16[8,2,14464]{2,1,0:T(2,128)(2,1)} %stack.2), calls=%async_computation | async-start | bytes 925696 | tf_op jit(solution)/shard_map/all_to_all | solution.py:42
  19.5 16.6 %all-to-all-done = bf16[8,2,14464]{2,1,0:T(2,128)(2,1)S(1)} async-done(((bf16[8,2,14464]{2,1,0:T(2,128)(2,1)}), bf16[8,2,14464]{2,1,0:T(2,128)(2,1)S(1)}, u32[]{:S(2)}, u32[]{:S(2)}) %all-to-all-start) | async-done | bytes 462880 | tf_op jit(solution)/shard_map/all_to_all | solution.py:42
  36.0 0.2 reshape.94
  36.4 0.2 reduce_window_sum.11
  37.1 0.2 multiply_convert_fusion
  37.5 2.0 convolution_convert_fusion
  39.6 92.2 %all_to_all.25 = bf16[32,16,7168]{2,1,0:T(8,128)(2,1)S(1)} all-to-all(bf16[32,16,7168]{2,1,0:T(8,128)(2,1)S(1)} %bitcast.122), channel_id=1, replica_groups=mesh['dp'=8,'expert'=32] {'expert'}, dimensions={0} | all-to-all | bytes 14680064 | tf_op jit(solution)/shard_map/all_to_all | solution.py:20
  131.8 2.1 fusion.6
  133.9 2.1 fusion.4
  135.9 3.1 fusion.1
  139.0 4.8 all-to-all-start.2
  144.1 44.9 %all-to-all-done.2 = bf16[32,8,7168]{2,1,0:T(8,128)(2,1)} async-done(((bf16[32,8,7168]{2,1,0:T(8,128)(2,1)}), bf16[32,8,7168]{2,1,0:T(8,128)(2,1)}, u32[]{:S(2)}, u32[]{:S(2)}) %all-to-all-start.2) | async-done | bytes 3670048 | tf_op jit(solution)/shard_map/all_to_all | solution.py:20
  189.0 3.6 fusion.14
  192.5 26.2 %all-reduce.6 = bf16[16,7168]{1,0:T(8,128)(2,1)S(1)} all-reduce(f32[16,7168]{1,0:T(8,128)S(1)} %fusion.14), channel_id=1, replica_groups=mesh['dp'=8,'expert'=32] {'dp'}, use_global_device_ids=true, to_apply=%region_4.5 | all-reduce | flops 114688 | bytes 688128 | tf_op jit(solution)/shard_map/psum | solution.py:107
  218.7 1.1 fusion.2
  219.9 58.5 %all_to_all.26 = bf16[32,8,7168]{2,1,0:T(8,128)(2,1)S(1)} all-to-all(bf16[32,8,7168]{2,1,0:T(8,128)(2,1)S(1)} %fusion.2), channel_id=1, replica_groups=mesh['dp'=8,'expert'=32] {'expert'}, dimensions={0} | all-to-all | bytes 7340032 | tf_op jit(solution)/shard_map/all_to_all | solution.py:20
  278.4 1.1 fusion.12
  279.5 0.9 copy-done.3
  280.4 1.2 fusion.19
  281.6 0.8 copy-done.5
  282.4 1.2 fusion.3
  283.6 48.9 %all_to_all.27 = bf16[32,8,7168]{2,1,0:T(8,128)(2,1)S(1)} all-to-all(bf16[32,8,7168]{2,1,0:T(8,128)(2,1)S(1)} %fusion.3), channel_id=1, replica_groups=mesh['dp'=8,'expert'=32] {'expert'}, dimensions={0} | all-to-all | bytes 7340032 | tf_op jit(solution)/shard_map/all_to_all | solution.py:20
  332.5 2.3 fusion.10
  334.9 0.6 dynamic-slice
  336.1 61.2 %all-reduce.5.cloned.1.call-done = f32[16,7168]{1,0:T(8,128)} async-done(((f32[16,7168]{1,0:T(8,128)}), f32[16,7168]{1,0:T(8,128)}) %all-reduce.5.cloned.1.call-update) | async-done | bytes 458768
  397.4 1.7 fusion.44
  399.1 80.1 %all-reduce.1 = (f32[]{:T(128)}, f32[]{:T(128)}, f32[]{:T(128)}) all-reduce(f32[]{:T(128)} %get-tuple-element.3, f32[]{:T(128)} %get-tuple-element.2, f32[]{:T(128)} %get-tuple-element.4), channel_id=1, replica_groups=mesh['dp'=8,'expert'=32] {'dp','expert'}, use_global_device_ids=true, to_apply=%region_7.8 | all-reduce | flops 3 | bytes 24 | tf_op jit(solution)/shard_map/psum | solution.py:127
  481.2 1.6 fusion.46
  (31 shorter events, 1.1 us)
Async XLA Ops:
  10.4 25.6 %all-to-all-start = ((bf16[8,2,14464]{2,1,0:T(2,128)(2,1)}), bf16[8,2,14464]{2,1,0:T(2,128)(2,1)S(1)}, u32[]{:S(2)}, u32[]{:S(2)}) async-start(bf16[8,2,14464]{2,1,0:T(2,128)(2,1)} %stack.2), calls=%async_computation | async-start | bytes 925696 | tf_op jit(solution)/shard_map/all_to_all | solution.py:42
  39.6 92.2 %copy-start.2 = (bf16[1,7168,256]{2,1,0:T(8,128)(2,1)S(1)}, bf16[1,7168,256]{2,1,0:T(8,128)(2,1)}, u32[]{:S(2)}) copy-start(bf16[1,7168,256]{2,1,0:T(8,128)(2,1)} %param.11) | copy-start | bytes 11010052
  131.8 2.1 copy-start.4
  133.8 2.1 copy-start
  139.0 50.0 %all-to-all-start.2 = ((bf16[32,8,7168]{2,1,0:T(8,128)(2,1)}), bf16[32,8,7168]{2,1,0:T(8,128)(2,1)}, u32[]{:S(2)}, u32[]{:S(2)}) async-start(bf16[32,8,7168]{2,1,0:T(8,128)(2,1)} %fusion.1), calls=%async_computation.2 | async-start | bytes 7340032 | tf_op jit(solution)/shard_map/all_to_all | solution.py:20
  143.8 253.6 %all-reduce.5.cloned.1.call-start = ((), (), s32[]{:S(2)}) async-start(), calls=%async_computation.5 | async-start | bytes 917504
  219.9 58.5 %copy-start.1 = (bf16[1,256,7168]{2,1,0:T(8,128)(2,1)S(1)}, bf16[1,256,7168]{2,1,0:T(8,128)(2,1)}, u32[]{:S(2)}) copy-start(bf16[1,256,7168]{2,1,0:T(8,128)(2,1)} %param.13) | copy-start | bytes 11010052
  278.4 2.0 copy-start.3
  280.4 2.0 copy-start.5
  332.5 2.4 copy-start.7
  332.5 64.8 %copy-start.6 = (bf16[1,2,7168]{2,1,0:T(2,128)(2,1)S(1)}, bf16[1,2,7168]{2,1,0:T(2,128)(2,1)}, u32[]{:S(2)}) copy-start(bf16[1,2,7168]{2,1,0:T(2,128)(2,1)} %param.8) | copy-start | bytes 86020
Sparse Core Ops, SparseCore 0:
  335.0 62.3 all-reduce.4
